TPU v7x, 256 devices: a whole 4x4x8 slice. The times are simulated.
256 devices in a mesh: pp: 8 (over x, core), ep: 32 (over z, y).
Axes of the slice: x: 4, y: 4, z: 8, core: 2. Of those that a mesh axis runs over, the one named last changes fastest.
Arguments:
- tokens: bfloat16 [512, 2048], P('ep'), may hold values from -6 to 6
- routes: int32 [8, 512, 8], P('pp'), may hold values from 0 to 31, all different within a row; in each aligned block of 16 rows (0 to 15, 16 to 31, ..., all dimensions but the last counted through in order) at most 5 rows name the same one
- combine: float32 [8, 512, 8], P('pp', 'ep'), may hold values from 0.05 to 0.5
- norm_gain: float32 [8, 2048], P('pp'), may hold values from 0.5 to 1.5
- expert_in: bfloat16 [8, 32, 2048, 1536], P('pp', 'ep'), may hold values from -0.125 to 0.125
- expert_out: bfloat16 [8, 32, 768, 2048], P('pp', 'ep'), may hold values from -0.21875 to 0.21875
Outputs:
- section_out: bfloat16 [8, 512, 2048], P('pp', 'ep')
Inputs may be any that keep to these rules, and one draw needn't show every extreme that they name: `routes`: each row names 8 different experts. Within the 16 rows of one device (rows i * 16 to (i + 1) * 16 - 1 of one layer) no expert is named more than 5 times, and some such block names some expert exactly 5 times.
All inputs are finite; a program needn't handle non-finite values.
Results may differ from a plain program's by a relative error of at most 0.028.
Values may be sent and summed in bfloat16 or wider, within the bound.
No kernel may reach another device: no remote copies, remote signals or barrier semaphores. Data moves between devices by JAX's collectives and lax.ppermute only.
A program may use at most 64 MiB of HBM per device.

v0:
```python
import jax
import jax.numpy as jnp
from jax import lax
from jax.sharding import PartitionSpec as P


def shards(tokens, routes, combine, norm_gain, expert_in, expert_out):
    group_size = lax.axis_size("ep")
    sections = lax.axis_size("pp")
    section_id = lax.axis_index("pp")
    member = lax.axis_index("ep")
    tok_dev, model_width = tokens.shape
    top_count = routes.shape[2]
    capacity = tok_dev * top_count * 5 // (4 * group_size)
    hidden_units = expert_out.shape[2]
    slot_count = group_size * capacity
    section_routes = routes[0]
    experts_axis = jnp.arange(group_size, dtype=jnp.int32)
    start_row = member * tok_dev
    own_routes = lax.dynamic_slice_in_dim(section_routes, start_row, tok_dev, 0)
    flat_routes = own_routes.reshape(-1)
    one_hot = (flat_routes[:, None] == experts_axis[None, :]).astype(jnp.int32)
    earlier = jnp.cumsum(one_hot, axis=0) - one_hot
    rank_of = jnp.sum(earlier * one_hot, axis=1)
    slot_of = flat_routes * capacity + rank_of
    slot_grid = slot_of[None, :] == jnp.arange(slot_count, dtype=jnp.int32)[:, None]
    slot_grid = slot_grid.reshape(slot_count, tok_dev, top_count)
    picker = jnp.any(slot_grid, axis=2).astype(jnp.bfloat16).reshape(group_size, capacity, tok_dev)
    weigher = jnp.sum(jnp.where(slot_grid, combine[0][None, :, :], 0.0), axis=2).T
    weigher = weigher.reshape(tok_dev, group_size, capacity)
    first_weights = expert_in[0, 0]
    second_weights = expert_out[0, 0]
    gain_row = norm_gain[0]

    lanes = 128 if model_width % 128 == 0 else model_width
    rows = model_width // lanes

    tiled_second = lax.optimization_barrier(second_weights.reshape(hidden_units, rows, lanes))

    def exchange(blocks):
        dense = blocks.reshape(group_size, capacity * rows, lanes)
        moved = lax.all_to_all(dense, "ep", 0, 0, tiled=True)
        return moved.reshape(blocks.shape)

    def layer(current):
        widened = current.astype(jnp.float32)
        scale = lax.rsqrt(jnp.mean(widened * widened, axis=-1, keepdims=True) + 1e-06)
        normed = (widened * scale * gain_row[None, :]).astype(jnp.bfloat16)
        packed = jnp.einsum(
            "gct,tjk->gcjk", picker, normed.reshape(tok_dev, rows, lanes), preferred_element_type=jnp.float32
        )
        arrived = exchange(packed.astype(jnp.bfloat16))
        projected = jnp.einsum(
            "gcjk,jkh->gch", arrived, first_weights.reshape(rows, lanes, -1), preferred_element_type=jnp.float32
        )
        hidden = (jax.nn.silu(projected[..., :hidden_units]) * projected[..., hidden_units:]).astype(
            jnp.bfloat16
        )
        produced = jnp.einsum("gch,hjk->gcjk", hidden, tiled_second, preferred_element_type=jnp.float32)
        returned = lax.all_to_all(
            produced.astype(jnp.bfloat16).reshape(group_size, capacity * rows, lanes), "ep", 0, 0, tiled=True
        )
        blended = jnp.einsum(
            "tgc,gcjk->tjk",
            weigher,
            returned.reshape(group_size, capacity, rows, lanes).astype(jnp.float32),
            precision=lax.Precision.HIGHEST,
        ).reshape(tok_dev, model_width)
        return (widened + blended).astype(jnp.bfloat16)

    def step(held):
        output = layer(held[0])
        return output, output

    current = tokens
    result = tokens
    for turn_index in range(sections):
        output, result = lax.cond(section_id == turn_index, step, lambda held: held, (current, result))
        if turn_index + 1 < sections:
            current = lax.ppermute(output, "pp", [(turn_index, turn_index + 1)])
    return result[None]


def solution(mesh):
    placed = (
        P("ep", None),
        P("pp", None, None),
        P("pp", "ep", None),
        P("pp", None),
        P("pp", "ep", None, None),
        P("pp", "ep", None, None),
    )
    return jax.shard_map(
        shards, mesh=mesh, in_specs=placed, out_specs=P("pp", "ep", None), check_vma=False
    )
```

profile of v0, /device:TPU:7, one launch (start us, length us, event | category | flops | bytes accessed | tf_op | source)
XLA Modules:
  0.0 412.1 jit_solution(1732477540427046199)
XLA Ops:
  0.0 0.8 constant_dynamic-slice_fusion
  0.8 0.1 copy.146
  0.8 0.1 eq.61
  0.9 0.1 fusion.154
  1.0 0.2 reduce_window_sum.11
  1.2 0.2 select_reduce_fusion.1
  1.4 0.1 reduce_sum.93
  1.4 0.1 copy.147
  1.5 0.8 bitcast_add_fusion
  2.3 0.1 copy.148
  2.4 0.8 copy.151
  3.1 0.1 fusion.153
  3.3 0.1 select_reduce_fusion
  3.4 0.1 copy.152
  3.5 0.1 copy.149
  3.7 0.0 copy-start
  3.7 0.0 copy-start.1
  3.7 3.2 copy.150
  6.9 0.0 copy-done
  6.9 0.0 copy-done.1
  7.0 0.0 copy-start.2
  7.0 0.6 copy-done.2
  7.6 0.7 collective-permute-start
  8.3 0.0 collective-permute-done
  8.3 0.7 collective-permute-start.1
  9.0 0.0 collective-permute-done.1
  9.0 0.2 conditional.10
  9.2 0.7 collective-permute-start.2
  9.9 0.0 collective-permute-done.2
  9.9 0.7 collective-permute-start.3
  10.6 0.0 collective-permute-done.3
  10.6 0.7 collective-permute-start.4
  11.3 0.0 collective-permute-done.4
  11.3 0.3 conditional.13
  11.6 0.7 collective-permute-start.5
  12.3 0.0 collective-permute-done.5
  12.3 1.3 collective-permute-start.6
  13.6 353.8 %collective-permute-done.6 = bf16[16,2048]{1,0:T(8,128)(2,1)S(1)} collective-permute-done((bf16[16,2048]{1,0:T(8,128)(2,1)S(1)}, bf16[16,2048]{1,0:T(8,128)(2,1)S(1)}, u32[]{:S(2)}, u32[]{:S(2)}) %collective-permute-start.6) | collective-permute-done | bytes 65568 | tf_op jit(solution)/shard_map/ppermute | solution.py:80
  367.4 44.7 %conditional.15 = (bf16[1,16,2048]{2,1,0:T(8,128)(2,1)}) conditional(s32[]{:T(128)} %convert_element_type.210, bf16[16,2048]{1,0:T(8,128)(2,1)} %get-tuple-element.209, (bf16[16,2048]{1,0:T(8,128)(2,1)S(1)}, f32[1,2048]{1,0:T(1,128)S(1)}, bf16[32,5,16]{2,1,0:T(8,128)(2,1)S(1)}, bf16[1,1,2048,1536]{3,2,1,0:T(8,128)(2,1)}, ...), branch_computations={%region_25.26_spmd, %region_26.28_spmd} | conditional | flops 1585070080 | bytes 22074664 | solution.py:78
  367.4 0.1 fusion.143
  367.5 0.1 fusion.148
  367.7 0.1 copy.174
  367.8 0.4 fusion.138
  368.1 0.3 copy.141
  368.4 18.0 %all_to_all.71 = bf16[32,80,128]{2,1,0:T(8,128)(2,1)S(1)} all-to-all(bf16[32,80,128]{2,1,0:T(8,128)(2,1)S(1)} %bitcast.388), channel_id=1, replica_groups=mesh['pp'=8,'ep'=32] {'ep'}, dimensions={0} | all-to-all | bytes 1310720 | tf_op jit(solution)/shard_map/cond/branch_1_fun/all_to_all | solution.py:42
  386.4 0.2 copy.142
  386.5 4.0 convolution_bitcast_fusion.14
  390.5 1.2 fusion.135
  391.7 1.1 copy.143
  392.8 4.4 %all-to-all-start.15 = ((bf16[32,80,128]{2,1,0:T(8,128)(2,1)}), bf16[32,80,128]{2,1,0:T(8,128)(2,1)S(1)}, u32[]{:S(2)}, u32[]{:S(2)}) async-start(bf16[32,80,128]{2,1,0:T(8,128)(2,1)} %copy.143), calls=%async_computation.15 | async-start | bytes 1310720 | tf_op jit(solution)/shard_map/cond/branch_1_fun/all_to_all | solution.py:60
  397.2 0.1 copy.176
  397.3 13.7 %all-to-all-done.15 = bf16[32,80,128]{2,1,0:T(8,128)(2,1)S(1)} async-done(((bf16[32,80,128]{2,1,0:T(8,128)(2,1)}), bf16[32,80,128]{2,1,0:T(8,128)(2,1)S(1)}, u32[]{:S(2)}, u32[]{:S(2)}) %all-to-all-start.15) | async-done | bytes 655392 | tf_op jit(solution)/shard_map/cond/branch_1_fun/all_to_all | solution.py:60
  411.0 0.4 convolution_bitcast_fusion.15
  411.4 0.7 fusion.147
  (11 shorter events, 0.1 us)
Async XLA Ops:
  3.7 3.3 copy-start
  3.7 3.3 copy-start.1
  7.0 0.6 copy-start.2
  7.6 0.7 collective-permute-start
  8.3 0.7 collective-permute-start.1
  9.2 0.7 collective-permute-start.2
  9.9 0.7 collective-permute-start.3
  10.6 0.7 collective-permute-start.4
  11.6 0.7 collective-permute-start.5
  12.3 355.1 %collective-permute-start.6 = (bf16[16,2048]{1,0:T(8,128)(2,1)S(1)}, bf16[16,2048]{1,0:T(8,128)(2,1)S(1)}, u32[]{:S(2)}, u32[]{:S(2)}) collective-permute-start(bf16[16,2048]{1,0:T(8,128)(2,1)S(1)} %get-tuple-element.210), channel_id=1, source_target_pairs={{192,224},{193,225},{194,226},{195,227},{196,228},{197,229},{198,2... | collective-permute-start | bytes 196616 | tf_op jit(solution)/shard_map/ppermute | solution.py:80
  392.8 18.2 %all-to-all-start.15 = ((bf16[32,80,128]{2,1,0:T(8,128)(2,1)}), bf16[32,80,128]{2,1,0:T(8,128)(2,1)S(1)}, u32[]{:S(2)}, u32[]{:S(2)}) async-start(bf16[32,80,128]{2,1,0:T(8,128)(2,1)} %copy.143), calls=%async_computation.15 | async-start | bytes 1310720 | tf_op jit(solution)/shard_map/cond/branch_1_fun/all_to_all | solution.py:60
where the time goes:
time: 413 us; the launch traced here: 412 us
  waiting for transfers between devices  368 us (89%)
  blocking collectives  18 us (4%)
  starting transfers between devices  9.65 us (2%)
  local copies, waits for them, and re-layouts  7.76 us (2%)
  matrix products  5.96 us (1%)
    ppermute x7, waiting for transfers between devices, shards(): current = lax.ppermute(output, 'pp', [(turn_index, turn_index + 1)])  354 us
    all_to_all x1, blocking collectives, exchange(): moved = lax.all_to_all(dense, 'ep', 0, 0, tiled=True)  18 us
    all_to_all x1, waiting for transfers between devices, layer(): lax.all_to_all(produced.astype(jnp.bfloat16).reshape(group_size, capacity...  13.7 us
  transfers between devices with their start and end apart: 8, of which 2 were waited for; matrix products, arithmetic and copies ran while one was open for 0% of the time, Pallas kernels for 0%

commit v1 on v0

--- a/solution.py
+++ b/solution.py
@@ -72,12 +72,13 @@
         output = layer(held[0])
         return output, output
 
-    current = tokens
-    result = tokens
-    for turn_index in range(sections):
-        output, result = lax.cond(section_id == turn_index, step, lambda held: held, (current, result))
-        if turn_index + 1 < sections:
-            current = lax.ppermute(output, "pp", [(turn_index, turn_index + 1)])
+    ring = [(i, i + 1) for i in range(sections - 1)]
+
+    def turn(turn_index, held):
+        output, result = lax.cond(section_id == turn_index, step, lambda kept: kept, held)
+        return lax.ppermute(output, "pp", ring), result
+
+    _, result = lax.fori_loop(0, sections, turn, (tokens, tokens))
     return result[None]
 
 

time: 413 us -> 398 us (0.964)
  waiting for transfers between devices: 368 us -> 334 us
  blocking collectives: 18 us -> 35.9 us
    ppermute x7 -> x8, waiting for transfers between devices: 354 us -> 334 us  [turn(): return (lax.ppermute(output, 'pp', ring), result)]
    all_to_all x0 -> x1, blocking collectives: none -> 18 us  [layer(): lax.all_to_all(produced.astype(jnp.bfloat16).reshape(group_size, capacity...]
    all_to_all x1 -> x0, waiting for transfers between devices: 13.7 us -> none  [layer(): lax.all_to_all(produced.astype(jnp.bfloat16).reshape(group_size, capacity...]
    ppermute x7 -> x8, starting transfers between devices: 5.27 us -> 10.3 us  [turn(): return (lax.ppermute(output, 'pp', ring), result)]
    all_to_all x1 -> x0, starting transfers between devices: 4.38 us -> none  [layer(): lax.all_to_all(produced.astype(jnp.bfloat16).reshape(group_size, capacity...]
  transfers between devices with their start and end apart: 8 -> 8, of which waited for: 2 -> 8; matrix products, arithmetic and copies ran while one was open for 0% -> 0% of each run, Pallas kernels for 0% -> 0%
where the time goes in v1:
time: 398 us
  waiting for transfers between devices  334 us (84%)
  blocking collectives  35.9 us (9%)
  starting transfers between devices  10.3 us (3%)
  local copies, waits for them, and re-layouts  9.9 us (2%)
  matrix products  5.63 us (1%)
    ppermute x8, waiting for transfers between devices, turn(): return (lax.ppermute(output, 'pp', ring), result)  334 us
    all_to_all x1, blocking collectives, layer(): lax.all_to_all(produced.astype(jnp.bfloat16).reshape(group_size, capacity...  18 us
    all_to_all x1, blocking collectives, exchange(): moved = lax.all_to_all(dense, 'ep', 0, 0, tiled=True)  18 us
    ppermute x8, starting transfers between devices, turn(): return (lax.ppermute(output, 'pp', ring), result)  10.3 us
  transfers between devices with their start and end apart: 8, of which 8 were waited for; matrix products, arithmetic and copies ran while one was open for 0% of the time, Pallas kernels for 0%

profile of v1, /device:TPU:7, one launch (start us, length us, event | category | flops | bytes accessed | tf_op | source)
XLA Modules:
  0.0 397.7 jit_solution(18361880076480752813)
XLA Ops:
  0.0 0.8 copy.70
  0.8 0.8 constant_dynamic-slice_fusion
  1.6 0.1 copy.32
  1.7 0.1 eq.36
  1.8 0.1 fusion.20
  1.9 0.2 reduce_window_sum.11
  2.0 0.2 select_reduce_fusion.1
  2.2 0.1 reduce_sum.30
  2.3 0.1 copy.33
  2.4 0.8 bitcast_add_fusion
  3.1 0.1 copy.34
  3.2 0.1 fusion.19
  3.4 0.1 copy.35
  3.5 0.1 copy.39
  3.6 3.2 copy.36
  6.8 0.0 copy-start.3
  6.8 0.0 copy-start.1
  6.8 2.8 copy.40
  9.6 0.0 copy-done.3
  9.6 0.1 copy.37
  9.7 0.1 select_reduce_fusion
  9.8 0.1 copy.38
  10.0 0.1 copy.41
  10.1 0.0 copy-done.1
  10.1 387.0 %while.15 = (s32[]{:T(128)}, bf16[16,2048]{1,0:T(8,128)(2,1)S(1)}, bf16[16,2048]{1,0:T(8,128)(2,1)S(1)}, s32[]{:T(128)}, f32[1,2048]{1,0:T(1,128)S(1)}, /*index=...) while((s32[]{:T(128)}, bf16[16,2048]{1,0:T(8,128)(2,1)S(1)}, ...), condition=%wide.region_8.9_spmd, body=%wide.region_4.8_spmd.sunk | while | flops 1585070080 | bytes 34496016 | solution.py:81
  10.1 1.3 collective-permute-start
  11.4 2.0 collective-permute-done
  13.4 1.3 collective-permute-start
  14.7 4.3 %collective-permute-done = bf16[16,2048]{1,0:T(8,128)(2,1)S(1)} collective-permute-done((bf16[16,2048]{1,0:T(8,128)(2,1)S(1)}, bf16[16,2048]{1,0:T(8,128)(2,1)S(1)}, u32[]{:S(2)}, u32[]{:S(2)}) %collective-permute-start) | collective-permute-done | bytes 65568 | tf_op jit(solution)/shard_map/while/body/eval_jaxpr/ppermute | solution.py:79
  19.0 1.3 collective-permute-start
  20.3 4.3 %collective-permute-done = bf16[16,2048]{1,0:T(8,128)(2,1)S(1)} collective-permute-done((bf16[16,2048]{1,0:T(8,128)(2,1)S(1)}, bf16[16,2048]{1,0:T(8,128)(2,1)S(1)}, u32[]{:S(2)}, u32[]{:S(2)}) %collective-permute-start) | collective-permute-done | bytes 65568 | tf_op jit(solution)/shard_map/while/body/eval_jaxpr/ppermute | solution.py:79
  24.6 1.3 collective-permute-start
  25.9 4.3 %collective-permute-done = bf16[16,2048]{1,0:T(8,128)(2,1)S(1)} collective-permute-done((bf16[16,2048]{1,0:T(8,128)(2,1)S(1)}, bf16[16,2048]{1,0:T(8,128)(2,1)S(1)}, u32[]{:S(2)}, u32[]{:S(2)}) %collective-permute-start) | collective-permute-done | bytes 65568 | tf_op jit(solution)/shard_map/while/body/eval_jaxpr/ppermute | solution.py:79
  30.2 1.3 collective-permute-start
  31.5 4.3 %collective-permute-done = bf16[16,2048]{1,0:T(8,128)(2,1)S(1)} collective-permute-done((bf16[16,2048]{1,0:T(8,128)(2,1)S(1)}, bf16[16,2048]{1,0:T(8,128)(2,1)S(1)}, u32[]{:S(2)}, u32[]{:S(2)}) %collective-permute-start) | collective-permute-done | bytes 65568 | tf_op jit(solution)/shard_map/while/body/eval_jaxpr/ppermute | solution.py:79
  35.8 1.3 collective-permute-start
  37.0 4.3 %collective-permute-done = bf16[16,2048]{1,0:T(8,128)(2,1)S(1)} collective-permute-done((bf16[16,2048]{1,0:T(8,128)(2,1)S(1)}, bf16[16,2048]{1,0:T(8,128)(2,1)S(1)}, u32[]{:S(2)}, u32[]{:S(2)}) %collective-permute-start) | collective-permute-done | bytes 65568 | tf_op jit(solution)/shard_map/while/body/eval_jaxpr/ppermute | solution.py:79
  41.3 1.3 collective-permute-start
  42.6 308.6 %collective-permute-done = bf16[16,2048]{1,0:T(8,128)(2,1)S(1)} collective-permute-done((bf16[16,2048]{1,0:T(8,128)(2,1)S(1)}, bf16[16,2048]{1,0:T(8,128)(2,1)S(1)}, u32[]{:S(2)}, u32[]{:S(2)}) %collective-permute-start) | collective-permute-done | bytes 65568 | tf_op jit(solution)/shard_map/while/body/eval_jaxpr/ppermute | solution.py:79
  351.2 42.6 %conditional.2 = ((bf16[16,2048]{1,0:T(8,128)(2,1)S(1)}, bf16[16,2048]{1,0:T(8,128)(2,1)S(1)})) conditional(s32[]{:T(128)} %convert_element_type.72, (bf16[16,2048]{1,0:T(8,128)(2,1)S(1)}, bf16[16,2048]{1,0:T(8,128)(2,1)S(1)}) %tuple.39, (bf16[16,2048]{1,0:T(8,128)(2,1)S(1)}, f32[1,2048]{1,0:T(1,128)S(1)}, bf16[32,5,16]{0,2,1:T(8,128)(2,1)S(1)}, ...), branch_computations={%region_5.5_spmd, %region_6.7_spmd} | conditional | flops 1585070080 | bytes 34102580 | solution.py:78
  351.2 0.1 fusion.10
  351.4 0.1 fusion.14
  351.5 0.4 fusion.5
  351.9 0.3 copy.27
  352.1 18.0 %all_to_all.8 = bf16[32,80,128]{2,1,0:T(8,128)(2,1)S(1)} all-to-all(bf16[32,80,128]{2,1,0:T(8,128)(2,1)S(1)} %bitcast.53), channel_id=1, replica_groups=mesh['pp'=8,'ep'=32] {'ep'}, dimensions={0} | all-to-all | bytes 1310720 | tf_op jit(solution)/shard_map/while/body/eval_jaxpr/cond/branch_1_fun/all_to_all | solution.py:42
  370.1 0.2 copy.28
  370.3 0.0 copy-start
  370.3 4.1 %convolution_bitcast_fusion = f32[32,5,1536]{2,0,1:T(8,128)S(1)} fusion(bf16[32,5,16,128]{3,0,2,1:T(8,128)(2,1)S(1)} %bitcast.55, bf16[16,128,1536,1]{2,1,0,3:T(8,128)(2,1)} %bitcast.52), kind=kOutput, calls=%fused_computation.2 | convolution fusion | flops 1006632960 | bytes 7929856 | tf_op jit(solution)/shard_map/while/body/eval_jaxpr/cond/branch_1_fun/gcjk,jkh->gch/dot_general | solution.py:53
  374.4 0.0 copy-done
  374.4 0.7 fusion.2
  375.2 0.3 copy.29
  375.4 18.0 %all_to_all.9 = bf16[32,80,128]{2,1,0:T(8,128)(2,1)S(1)} all-to-all(bf16[32,80,128]{2,1,0:T(8,128)(2,1)S(1)} %copy.29), channel_id=1, replica_groups=mesh['pp'=8,'ep'=32] {'ep'}, dimensions={0} | all-to-all | bytes 1310720 | tf_op jit(solution)/shard_map/while/body/eval_jaxpr/cond/branch_1_fun/all_to_all | solution.py:60
  393.4 0.4 convolution_bitcast_fusion.1
  393.9 1.3 collective-permute-start
  395.2 1.8 collective-permute-done
  397.0 0.0 copy-start.2
  397.0 0.6 copy-done.2
  (23 shorter events, 0.2 us)
Async XLA Ops:
  6.8 2.8 copy-start.3
  6.8 3.2 copy-start.1
  10.1 3.3 collective-permute-start
  13.4 5.6 %collective-permute-start = (bf16[16,2048]{1,0:T(8,128)(2,1)S(1)}, bf16[16,2048]{1,0:T(8,128)(2,1)S(1)}, u32[]{:S(2)}, u32[]{:S(2)}) collective-permute-start(bf16[16,2048]{1,0:T(8,128)(2,1)S(1)} %get-tuple-element.279), channel_id=1, source_target_pairs={{0,32},{32,64},{64,96},{96,128},{128,160},{160,192},{192,224},{1,3... | collective-permute-start | bytes 196616 | tf_op jit(solution)/shard_map/while/body/eval_jaxpr/ppermute | solution.py:79
  19.0 5.6 %collective-permute-start = (bf16[16,2048]{1,0:T(8,128)(2,1)S(1)}, bf16[16,2048]{1,0:T(8,128)(2,1)S(1)}, u32[]{:S(2)}, u32[]{:S(2)}) collective-permute-start(bf16[16,2048]{1,0:T(8,128)(2,1)S(1)} %get-tuple-element.279), channel_id=1, source_target_pairs={{0,32},{32,64},{64,96},{96,128},{128,160},{160,192},{192,224},{1,3... | collective-permute-start | bytes 196616 | tf_op jit(solution)/shard_map/while/body/eval_jaxpr/ppermute | solution.py:79
  24.6 5.6 %collective-permute-start = (bf16[16,2048]{1,0:T(8,128)(2,1)S(1)}, bf16[16,2048]{1,0:T(8,128)(2,1)S(1)}, u32[]{:S(2)}, u32[]{:S(2)}) collective-permute-start(bf16[16,2048]{1,0:T(8,128)(2,1)S(1)} %get-tuple-element.279), channel_id=1, source_target_pairs={{0,32},{32,64},{64,96},{96,128},{128,160},{160,192},{192,224},{1,3... | collective-permute-start | bytes 196616 | tf_op jit(solution)/shard_map/while/body/eval_jaxpr/ppermute | solution.py:79
  30.2 5.6 %collective-permute-start = (bf16[16,2048]{1,0:T(8,128)(2,1)S(1)}, bf16[16,2048]{1,0:T(8,128)(2,1)S(1)}, u32[]{:S(2)}, u32[]{:S(2)}) collective-permute-start(bf16[16,2048]{1,0:T(8,128)(2,1)S(1)} %get-tuple-element.279), channel_id=1, source_target_pairs={{0,32},{32,64},{64,96},{96,128},{128,160},{160,192},{192,224},{1,3... | collective-permute-start | bytes 196616 | tf_op jit(solution)/shard_map/while/body/eval_jaxpr/ppermute | solution.py:79
  35.8 5.6 %collective-permute-start = (bf16[16,2048]{1,0:T(8,128)(2,1)S(1)}, bf16[16,2048]{1,0:T(8,128)(2,1)S(1)}, u32[]{:S(2)}, u32[]{:S(2)}) collective-permute-start(bf16[16,2048]{1,0:T(8,128)(2,1)S(1)} %get-tuple-element.279), channel_id=1, source_target_pairs={{0,32},{32,64},{64,96},{96,128},{128,160},{160,192},{192,224},{1,3... | collective-permute-start | bytes 196616 | tf_op jit(solution)/shard_map/while/body/eval_jaxpr/ppermute | solution.py:79
  41.3 309.9 %collective-permute-start = (bf16[16,2048]{1,0:T(8,128)(2,1)S(1)}, bf16[16,2048]{1,0:T(8,128)(2,1)S(1)}, u32[]{:S(2)}, u32[]{:S(2)}) collective-permute-start(bf16[16,2048]{1,0:T(8,128)(2,1)S(1)} %get-tuple-element.279), channel_id=1, source_target_pairs={{0,32},{32,64},{64,96},{96,128},{128,160},{160,192},{192,224},{1,3... | collective-permute-start | bytes 196616 | tf_op jit(solution)/shard_map/while/body/eval_jaxpr/ppermute | solution.py:79
  370.3 4.1 %copy-start = (bf16[768,16,128]{2,0,1:T(8,128)(2,1)S(1)}, bf16[768,16,128]{2,0,1:T(8,128)(2,1)}, u32[]{:S(2)}) copy-start(bf16[768,16,128]{2,0,1:T(8,128)(2,1)} %get-tuple-element.170) | copy-start | bytes 9437188 | tf_op jit(solution)/shard_map/while/body/eval_jaxpr/cond
  393.9 3.1 collective-permute-start
  397.0 0.6 copy-start.2

commit v2 on v1

--- a/solution.py
+++ b/solution.py
@@ -35,14 +35,12 @@
     lanes = 128 if model_width % 128 == 0 else model_width
     rows = model_width // lanes
 
-    tiled_second = lax.optimization_barrier(second_weights.reshape(hidden_units, rows, lanes))
-
     def exchange(blocks):
         dense = blocks.reshape(group_size, capacity * rows, lanes)
         moved = lax.all_to_all(dense, "ep", 0, 0, tiled=True)
         return moved.reshape(blocks.shape)
 
-    def layer(current):
+    def layer(current, down_weights):
         widened = current.astype(jnp.float32)
         scale = lax.rsqrt(jnp.mean(widened * widened, axis=-1, keepdims=True) + 1e-06)
         normed = (widened * scale * gain_row[None, :]).astype(jnp.bfloat16)
@@ -56,7 +54,7 @@
         hidden = (jax.nn.silu(projected[..., :hidden_units]) * projected[..., hidden_units:]).astype(
             jnp.bfloat16
         )
-        produced = jnp.einsum("gch,hjk->gcjk", hidden, tiled_second, preferred_element_type=jnp.float32)
+        produced = jnp.einsum("gch,hjk->gcjk", hidden, down_weights, preferred_element_type=jnp.float32)
         returned = lax.all_to_all(
             produced.astype(jnp.bfloat16).reshape(group_size, capacity * rows, lanes), "ep", 0, 0, tiled=True
         )
@@ -68,17 +66,26 @@
         ).reshape(tok_dev, model_width)
         return (widened + blended).astype(jnp.bfloat16)
 
-    def step(held):
-        output = layer(held[0])
+    ring = [(i, i + 1) for i in range(sections - 1)]
+    plain_second = second_weights.reshape(hidden_units, rows, lanes)
+
+    def first_step(held):
+        output = layer(held[0], plain_second)
         return output, output
 
-    ring = [(i, i + 1) for i in range(sections - 1)]
+    output, result = lax.cond(section_id == 0, first_step, lambda kept: kept, (tokens, tokens))
+    current = lax.ppermute(output, "pp", ring)
+    tiled_second, current = lax.optimization_barrier((plain_second, current))
+
+    def step(held):
+        output = layer(held[0], tiled_second)
+        return output, output
 
     def turn(turn_index, held):
         output, result = lax.cond(section_id == turn_index, step, lambda kept: kept, held)
         return lax.ppermute(output, "pp", ring), result
 
-    _, result = lax.fori_loop(0, sections, turn, (tokens, tokens))
+    _, result = lax.fori_loop(1, sections, turn, (current, result))
     return result[None]
 
 

time: 398 us -> 401 us (level)
    ppermute x8 -> x7, starting transfers between devices: 10.3 us -> 8.98 us  [turn(): return (lax.ppermute(output, 'pp', ring), result)]
    ppermute x8 -> x7, waiting for transfers between devices: 334 us -> 334 us  [turn(): return (lax.ppermute(output, 'pp', ring), result)]
where the time goes in v2:
time: 401 us; the launch traced here: 400 us
  waiting for transfers between devices  336 us (84%)
  blocking collectives  35.9 us (9%)
  local copies, waits for them, and re-layouts  10.4 us (3%)
  starting transfers between devices  10.3 us (3%)
  matrix products  5.6 us (1%)
    ppermute x7, waiting for transfers between devices, turn(): return (lax.ppermute(output, 'pp', ring), result)  334 us
    all_to_all x1, blocking collectives, layer(): lax.all_to_all(produced.astype(jnp.bfloat16).reshape(group_size, capacity...  18 us
    all_to_all x1, blocking collectives, exchange(): moved = lax.all_to_all(dense, 'ep', 0, 0, tiled=True)  18 us
    ppermute x7, starting transfers between devices, turn(): return (lax.ppermute(output, 'pp', ring), result)  8.98 us
  transfers between devices with their start and end apart: 8, of which 8 were waited for; matrix products, arithmetic and copies ran while one was open for 0% of the time, Pallas kernels for 0%

profile of v2, /device:TPU:7, one launch (start us, length us, event | category | flops | bytes accessed | tf_op | source)
XLA Modules:
  0.0 400.4 jit_solution(969257966771366149)
XLA Ops:
  0.0 0.8 constant_dynamic-slice_fusion
  0.8 0.1 copy.49
  0.8 0.1 eq.40
  0.9 0.8 copy.53
  1.7 0.1 fusion.39
  1.8 0.2 reduce_window_sum.11
  1.9 0.2 select_reduce_fusion.1
  2.1 0.1 reduce_sum.39
  2.2 0.1 copy.50
  2.3 0.8 bitcast_add_fusion
  3.1 0.1 copy.51
  3.1 0.1 fusion.38
  3.3 0.1 select_reduce_fusion
  3.4 0.1 copy.52
  3.6 0.1 copy.54
  3.7 0.0 copy-start.1
  3.7 0.0 copy-start.2
  3.7 3.2 copy.48
  6.9 0.0 copy-done.1
  6.9 0.0 copy-done.2
  7.0 0.0 copy-start.3
  7.0 0.6 copy-done.3
  7.6 1.3 collective-permute-start.1
  8.9 0.1 copy.58
  9.0 0.1 copy.60
  9.1 0.0 copy-start.4
  9.1 1.8 collective-permute-done.1
  10.9 2.8 copy.59
  13.7 0.0 copy-done.4
  13.7 386.0 %while.15 = (s32[]{:T(128)}, bf16[16,2048]{1,0:T(8,128)(2,1)S(1)}, bf16[16,2048]{1,0:T(8,128)(2,1)S(1)}, s32[]{:T(128)}, f32[1,2048]{1,0:T(1,128)S(1)}, /*index=...) while((s32[]{:T(128)}, bf16[16,2048]{1,0:T(8,128)(2,1)S(1)}, ...), condition=%wide.region_11.12_spmd, body=%wide.region_7.11_spmd.sunk | while | flops 1585070080 | bytes 34496016 | solution.py:88
  13.7 1.3 collective-permute-start
  15.0 4.3 %collective-permute-done = bf16[16,2048]{1,0:T(8,128)(2,1)S(1)} collective-permute-done((bf16[16,2048]{1,0:T(8,128)(2,1)S(1)}, bf16[16,2048]{1,0:T(8,128)(2,1)S(1)}, u32[]{:S(2)}, u32[]{:S(2)}) %collective-permute-start) | collective-permute-done | bytes 65568 | tf_op jit(solution)/shard_map/while/body/eval_jaxpr/ppermute | solution.py:86
  19.3 1.3 collective-permute-start
  20.6 4.3 %collective-permute-done = bf16[16,2048]{1,0:T(8,128)(2,1)S(1)} collective-permute-done((bf16[16,2048]{1,0:T(8,128)(2,1)S(1)}, bf16[16,2048]{1,0:T(8,128)(2,1)S(1)}, u32[]{:S(2)}, u32[]{:S(2)}) %collective-permute-start) | collective-permute-done | bytes 65568 | tf_op jit(solution)/shard_map/while/body/eval_jaxpr/ppermute | solution.py:86
  24.9 1.3 collective-permute-start
  26.2 4.3 %collective-permute-done = bf16[16,2048]{1,0:T(8,128)(2,1)S(1)} collective-permute-done((bf16[16,2048]{1,0:T(8,128)(2,1)S(1)}, bf16[16,2048]{1,0:T(8,128)(2,1)S(1)}, u32[]{:S(2)}, u32[]{:S(2)}) %collective-permute-start) | collective-permute-done | bytes 65568 | tf_op jit(solution)/shard_map/while/body/eval_jaxpr/ppermute | solution.py:86
  30.5 1.3 collective-permute-start
  31.8 4.3 %collective-permute-done = bf16[16,2048]{1,0:T(8,128)(2,1)S(1)} collective-permute-done((bf16[16,2048]{1,0:T(8,128)(2,1)S(1)}, bf16[16,2048]{1,0:T(8,128)(2,1)S(1)}, u32[]{:S(2)}, u32[]{:S(2)}) %collective-permute-start) | collective-permute-done | bytes 65568 | tf_op jit(solution)/shard_map/while/body/eval_jaxpr/ppermute | solution.py:86
  36.0 1.3 collective-permute-start
  37.3 4.3 %collective-permute-done = bf16[16,2048]{1,0:T(8,128)(2,1)S(1)} collective-permute-done((bf16[16,2048]{1,0:T(8,128)(2,1)S(1)}, bf16[16,2048]{1,0:T(8,128)(2,1)S(1)}, u32[]{:S(2)}, u32[]{:S(2)}) %collective-permute-start) | collective-permute-done | bytes 65568 | tf_op jit(solution)/shard_map/while/body/eval_jaxpr/ppermute | solution.py:86
  41.6 1.3 collective-permute-start
  42.9 311.1 %collective-permute-done = bf16[16,2048]{1,0:T(8,128)(2,1)S(1)} collective-permute-done((bf16[16,2048]{1,0:T(8,128)(2,1)S(1)}, bf16[16,2048]{1,0:T(8,128)(2,1)S(1)}, u32[]{:S(2)}, u32[]{:S(2)}) %collective-permute-start) | collective-permute-done | bytes 65568 | tf_op jit(solution)/shard_map/while/body/eval_jaxpr/ppermute | solution.py:86
  354.0 42.6 %conditional.4 = ((bf16[16,2048]{1,0:T(8,128)(2,1)S(1)}, bf16[16,2048]{1,0:T(8,128)(2,1)S(1)})) conditional(s32[]{:T(128)} %convert_element_type.123, (bf16[16,2048]{1,0:T(8,128)(2,1)S(1)}, bf16[16,2048]{1,0:T(8,128)(2,1)S(1)}) %tuple.53, (bf16[16,2048]{1,0:T(8,128)(2,1)S(1)}, f32[1,2048]{1,0:T(1,128)S(1)}, bf16[32,5,16]{0,2,1:T(8,128)(2,1)S(1)}, ...), branch_computations={%region_8.8_spmd, %region_9.10_spmd} | conditional | flops 1585070080 | bytes 34102580 | solution.py:85
  354.0 0.1 fusion.29
  354.1 0.1 fusion.33
  354.3 0.4 fusion.24
  354.6 0.3 copy.43
  354.9 18.0 %all_to_all.17 = bf16[32,80,128]{2,1,0:T(8,128)(2,1)S(1)} all-to-all(bf16[32,80,128]{2,1,0:T(8,128)(2,1)S(1)} %bitcast.98), channel_id=1, replica_groups=mesh['pp'=8,'ep'=32] {'ep'}, dimensions={0} | all-to-all | bytes 1310720 | tf_op jit(solution)/shard_map/while/body/eval_jaxpr/cond/branch_1_fun/all_to_all | solution.py:40
  372.9 0.2 copy.44
  373.0 0.0 copy-start
  373.0 4.1 %convolution_bitcast_fusion.2 = f32[32,5,1536]{2,0,1:T(8,128)S(1)} fusion(bf16[32,5,16,128]{3,0,2,1:T(8,128)(2,1)S(1)} %bitcast.100, bf16[16,128,1536,1]{2,1,0,3:T(8,128)(2,1)} %bitcast.97), kind=kOutput, calls=%fused_computation.26 | convolution fusion | flops 1006632960 | bytes 7929856 | tf_op jit(solution)/shard_map/while/body/eval_jaxpr/cond/branch_1_fun/gcjk,jkh->gch/dot_general | solution.py:51
  377.2 0.0 copy-done
  377.2 0.7 fusion.21
  377.9 0.3 copy.45
  378.2 18.0 %all_to_all.18 = bf16[32,80,128]{2,1,0:T(8,128)(2,1)S(1)} all-to-all(bf16[32,80,128]{2,1,0:T(8,128)(2,1)S(1)} %copy.45), channel_id=1, replica_groups=mesh['pp'=8,'ep'=32] {'ep'}, dimensions={0} | all-to-all | bytes 1310720 | tf_op jit(solution)/shard_map/while/body/eval_jaxpr/cond/branch_1_fun/all_to_all | solution.py:58
  396.1 0.4 convolution_bitcast_fusion.3
  396.6 1.3 collective-permute-start
  397.9 1.8 collective-permute-done
  399.8 0.0 copy-start.5
  399.8 0.6 copy-done.5
  (22 shorter events, 0.2 us)
Async XLA Ops:
  3.7 3.2 copy-start.1
  3.7 3.2 copy-start.2
  7.0 0.6 copy-start.3
  7.6 3.3 collective-permute-start.1
  9.1 4.6 %copy-start.4 = (bf16[16,2048]{1,0:T(8,128)(2,1)S(1)}, bf16[16,2048]{1,0:T(8,128)(2,1)}, u32[]{:S(2)}) copy-start(bf16[16,2048]{1,0:T(8,128)(2,1)} %copy-done.3) | copy-start | bytes 196612
  13.7 5.6 %collective-permute-start = (bf16[16,2048]{1,0:T(8,128)(2,1)S(1)}, bf16[16,2048]{1,0:T(8,128)(2,1)S(1)}, u32[]{:S(2)}, u32[]{:S(2)}) collective-permute-start(bf16[16,2048]{1,0:T(8,128)(2,1)S(1)} %get-tuple-element.318), channel_id=1, source_target_pairs={{0,32},{32,64},{64,96},{96,128},{128,160},{160,192},{192,224},{1,3... | collective-permute-start | bytes 196616 | tf_op jit(solution)/shard_map/while/body/eval_jaxpr/ppermute | solution.py:86
  19.3 5.6 %collective-permute-start = (bf16[16,2048]{1,0:T(8,128)(2,1)S(1)}, bf16[16,2048]{1,0:T(8,128)(2,1)S(1)}, u32[]{:S(2)}, u32[]{:S(2)}) collective-permute-start(bf16[16,2048]{1,0:T(8,128)(2,1)S(1)} %get-tuple-element.318), channel_id=1, source_target_pairs={{0,32},{32,64},{64,96},{96,128},{128,160},{160,192},{192,224},{1,3... | collective-permute-start | bytes 196616 | tf_op jit(solution)/shard_map/while/body/eval_jaxpr/ppermute | solution.py:86
  24.9 5.6 %collective-permute-start = (bf16[16,2048]{1,0:T(8,128)(2,1)S(1)}, bf16[16,2048]{1,0:T(8,128)(2,1)S(1)}, u32[]{:S(2)}, u32[]{:S(2)}) collective-permute-start(bf16[16,2048]{1,0:T(8,128)(2,1)S(1)} %get-tuple-element.318), channel_id=1, source_target_pairs={{0,32},{32,64},{64,96},{96,128},{128,160},{160,192},{192,224},{1,3... | collective-permute-start | bytes 196616 | tf_op jit(solution)/shard_map/while/body/eval_jaxpr/ppermute | solution.py:86
  30.5 5.6 %collective-permute-start = (bf16[16,2048]{1,0:T(8,128)(2,1)S(1)}, bf16[16,2048]{1,0:T(8,128)(2,1)S(1)}, u32[]{:S(2)}, u32[]{:S(2)}) collective-permute-start(bf16[16,2048]{1,0:T(8,128)(2,1)S(1)} %get-tuple-element.318), channel_id=1, source_target_pairs={{0,32},{32,64},{64,96},{96,128},{128,160},{160,192},{192,224},{1,3... | collective-permute-start | bytes 196616 | tf_op jit(solution)/shard_map/while/body/eval_jaxpr/ppermute | solution.py:86
  36.0 5.6 %collective-permute-start = (bf16[16,2048]{1,0:T(8,128)(2,1)S(1)}, bf16[16,2048]{1,0:T(8,128)(2,1)S(1)}, u32[]{:S(2)}, u32[]{:S(2)}) collective-permute-start(bf16[16,2048]{1,0:T(8,128)(2,1)S(1)} %get-tuple-element.318), channel_id=1, source_target_pairs={{0,32},{32,64},{64,96},{96,128},{128,160},{160,192},{192,224},{1,3... | collective-permute-start | bytes 196616 | tf_op jit(solution)/shard_map/while/body/eval_jaxpr/ppermute | solution.py:86
  41.6 312.4 %collective-permute-start = (bf16[16,2048]{1,0:T(8,128)(2,1)S(1)}, bf16[16,2048]{1,0:T(8,128)(2,1)S(1)}, u32[]{:S(2)}, u32[]{:S(2)}) collective-permute-start(bf16[16,2048]{1,0:T(8,128)(2,1)S(1)} %get-tuple-element.318), channel_id=1, source_target_pairs={{0,32},{32,64},{64,96},{96,128},{128,160},{160,192},{192,224},{1,3... | collective-permute-start | bytes 196616 | tf_op jit(solution)/shard_map/while/body/eval_jaxpr/ppermute | solution.py:86
  373.0 4.1 %copy-start = (bf16[768,16,128]{2,0,1:T(8,128)(2,1)S(1)}, bf16[768,16,128]{2,0,1:T(8,128)(2,1)}, u32[]{:S(2)}) copy-start(bf16[768,16,128]{2,0,1:T(8,128)(2,1)} %get-tuple-element.189) | copy-start | bytes 9437188 | tf_op jit(solution)/shard_map/while/body/eval_jaxpr/cond
  396.6 3.1 collective-permute-start
  399.8 0.6 copy-start.5

commit v3 on v1

--- a/solution.py
+++ b/solution.py
@@ -78,7 +78,8 @@
         output, result = lax.cond(section_id == turn_index, step, lambda kept: kept, held)
         return lax.ppermute(output, "pp", ring), result
 
-    _, result = lax.fori_loop(0, sections, turn, (tokens, tokens))
+    held = lax.fori_loop(0, sections - 1, turn, (tokens, tokens))
+    _, result = lax.cond(section_id == sections - 1, step, lambda kept: kept, held)
     return result[None]
 
 

time: 398 us -> 402 us (1.010)
  blocking collectives: 35.9 us -> 18 us
  waiting for transfers between devices: 334 us -> 350 us
    all_to_all x1 -> x0, blocking collectives: 18 us -> none  [layer(): lax.all_to_all(produced.astype(jnp.bfloat16).reshape(group_size, capacity...]
    all_to_all x0 -> x1, waiting for transfers between devices: none -> 13.7 us  [layer(): lax.all_to_all(produced.astype(jnp.bfloat16).reshape(group_size, capacity...]
    all_to_all x0 -> x1, starting transfers between devices: none -> 4.39 us  [layer(): lax.all_to_all(produced.astype(jnp.bfloat16).reshape(group_size, capacity...]
    ppermute x8 -> x7, waiting for transfers between devices: 334 us -> 336 us  [turn(): return (lax.ppermute(output, 'pp', ring), result)]
    ppermute x8 -> x7, starting transfers between devices: 10.3 us -> 8.96 us  [turn(): return (lax.ppermute(output, 'pp', ring), result)]
where the time goes in v3:
time: 402 us; the launch traced here: 401 us
  waiting for transfers between devices  350 us (87%)
  blocking collectives  18 us (4%)
  starting transfers between devices  13.4 us (3%)
  local copies, waits for them, and re-layouts  11.6 us (3%)
  matrix products  5.96 us (1%)
    ppermute x7, waiting for transfers between devices, turn(): return (lax.ppermute(output, 'pp', ring), result)  336 us
    all_to_all x1, blocking collectives, exchange(): moved = lax.all_to_all(dense, 'ep', 0, 0, tiled=True)  18 us
    all_to_all x1, waiting for transfers between devices, layer(): lax.all_to_all(produced.astype(jnp.bfloat16).reshape(group_size, capacity...  13.7 us
    ppermute x7, starting transfers between devices, turn(): return (lax.ppermute(output, 'pp', ring), result)  8.96 us
  transfers between devices with their start and end apart: 8, of which 8 were waited for; matrix products, arithmetic and copies ran while one was open for 0% of the time, Pallas kernels for 0%

profile of v3, /device:TPU:7, one launch (start us, length us, event | category | flops | bytes accessed | tf_op | source)
XLA Modules:
  0.0 401.2 jit_solution(11619942687395436025)
XLA Ops:
  0.0 0.8 copy.111
  0.8 0.8 constant_dynamic-slice_fusion
  1.6 0.1 copy.50
  1.7 0.1 eq.40
  1.8 0.1 fusion.40
  1.9 0.2 reduce_window_sum.11
  2.0 0.2 select_reduce_fusion.1
  2.2 0.1 reduce_sum.39
  2.3 0.1 copy.51
  2.4 0.8 bitcast_add_fusion
  3.1 0.1 copy.52
  3.2 0.8 copy.55
  4.0 0.1 select_reduce_fusion
  4.1 0.1 copy.56
  4.2 0.1 copy.59
  4.3 0.1 fusion.39
  4.5 0.1 copy.53
  4.6 0.1 copy.57
  4.7 3.2 copy.54
  7.9 0.0 copy-start.1
  7.9 2.8 copy.58
  10.7 0.6 copy.99
  11.4 0.0 copy-done.1
  11.4 345.2 %while.18 = (s32[]{:T(128)}, bf16[16,2048]{1,0:T(8,128)(2,1)S(1)}, bf16[16,2048]{1,0:T(8,128)(2,1)}, s32[]{:T(128)}, f32[1,2048]{1,0:T(1,128)S(1)}, /*index=5*/b...) while((s32[]{:T(128)}, bf16[16,2048]{1,0:T(8,128)(2,1)S(1)}, ...), condition=%wide.region_8.9_spmd, body=%wide.region_4.8_spmd.sunk | while | flops 1585070080 | bytes 34496016 | solution.py:81
  11.4 1.3 collective-permute-start
  12.7 2.0 collective-permute-done
  14.7 1.3 collective-permute-start
  16.0 4.3 %collective-permute-done = bf16[16,2048]{1,0:T(8,128)(2,1)S(1)} collective-permute-done((bf16[16,2048]{1,0:T(8,128)(2,1)S(1)}, bf16[16,2048]{1,0:T(8,128)(2,1)S(1)}, u32[]{:S(2)}, u32[]{:S(2)}) %collective-permute-start) | collective-permute-done | bytes 65568 | tf_op jit(solution)/shard_map/while/body/eval_jaxpr/ppermute | solution.py:79
  20.3 1.3 collective-permute-start
  21.6 4.3 %collective-permute-done = bf16[16,2048]{1,0:T(8,128)(2,1)S(1)} collective-permute-done((bf16[16,2048]{1,0:T(8,128)(2,1)S(1)}, bf16[16,2048]{1,0:T(8,128)(2,1)S(1)}, u32[]{:S(2)}, u32[]{:S(2)}) %collective-permute-start) | collective-permute-done | bytes 65568 | tf_op jit(solution)/shard_map/while/body/eval_jaxpr/ppermute | solution.py:79
  25.9 1.3 collective-permute-start
  27.1 4.3 %collective-permute-done = bf16[16,2048]{1,0:T(8,128)(2,1)S(1)} collective-permute-done((bf16[16,2048]{1,0:T(8,128)(2,1)S(1)}, bf16[16,2048]{1,0:T(8,128)(2,1)S(1)}, u32[]{:S(2)}, u32[]{:S(2)}) %collective-permute-start) | collective-permute-done | bytes 65568 | tf_op jit(solution)/shard_map/while/body/eval_jaxpr/ppermute | solution.py:79
  31.4 1.3 collective-permute-start
  32.7 4.3 %collective-permute-done = bf16[16,2048]{1,0:T(8,128)(2,1)S(1)} collective-permute-done((bf16[16,2048]{1,0:T(8,128)(2,1)S(1)}, bf16[16,2048]{1,0:T(8,128)(2,1)S(1)}, u32[]{:S(2)}, u32[]{:S(2)}) %collective-permute-start) | collective-permute-done | bytes 65568 | tf_op jit(solution)/shard_map/while/body/eval_jaxpr/ppermute | solution.py:79
  37.0 1.3 collective-permute-start
  38.3 4.3 %collective-permute-done = bf16[16,2048]{1,0:T(8,128)(2,1)S(1)} collective-permute-done((bf16[16,2048]{1,0:T(8,128)(2,1)S(1)}, bf16[16,2048]{1,0:T(8,128)(2,1)S(1)}, u32[]{:S(2)}, u32[]{:S(2)}) %collective-permute-start) | collective-permute-done | bytes 65568 | tf_op jit(solution)/shard_map/while/body/eval_jaxpr/ppermute | solution.py:79
  42.6 1.3 collective-permute-start
  43.9 312.6 %collective-permute-done = bf16[16,2048]{1,0:T(8,128)(2,1)S(1)} collective-permute-done((bf16[16,2048]{1,0:T(8,128)(2,1)S(1)}, bf16[16,2048]{1,0:T(8,128)(2,1)S(1)}, u32[]{:S(2)}, u32[]{:S(2)}) %collective-permute-start) | collective-permute-done | bytes 65568 | tf_op jit(solution)/shard_map/while/body/eval_jaxpr/ppermute | solution.py:79
  356.5 44.7 %conditional.2 = (bf16[1,16,2048]{2,1,0:T(8,128)(2,1)}) conditional(s32[]{:T(128)} %convert_element_type.64, bf16[16,2048]{1,0:T(8,128)(2,1)} %get-tuple-element.210, (bf16[16,2048]{1,0:T(8,128)(2,1)S(1)}, f32[1,2048]{1,0:T(1,128)S(1)}, bf16[32,5,16]{2,1,0:T(8,128)(2,1)S(1)}, bf16[1,1,2048,1536]{3,2,1,0:T(8,128)(2,1)}, ...), branch_computations={%region_9.10_spmd, %region_10.12_spmd} | conditional | flops 1585070080 | bytes 22074664 | solution.py:82
  356.5 0.1 fusion.29
  356.7 0.1 fusion.34
  356.8 0.1 copy.60
  356.9 0.4 fusion.24
  357.3 0.3 copy.45
  357.5 18.0 %all_to_all.18 = bf16[32,80,128]{2,1,0:T(8,128)(2,1)S(1)} all-to-all(bf16[32,80,128]{2,1,0:T(8,128)(2,1)S(1)} %bitcast.110), channel_id=1, replica_groups=mesh['pp'=8,'ep'=32] {'ep'}, dimensions={0} | all-to-all | bytes 1310720 | tf_op jit(solution)/shard_map/cond/branch_1_fun/all_to_all | solution.py:42
  375.5 0.2 copy.46
  375.7 4.0 convolution_bitcast_fusion.2
  379.7 1.2 fusion.21
  380.9 1.1 copy.47
  382.0 4.4 %all-to-all-start.3 = ((bf16[32,80,128]{2,1,0:T(8,128)(2,1)}), bf16[32,80,128]{2,1,0:T(8,128)(2,1)S(1)}, u32[]{:S(2)}, u32[]{:S(2)}) async-start(bf16[32,80,128]{2,1,0:T(8,128)(2,1)} %copy.47), calls=%async_computation.3 | async-start | bytes 1310720 | tf_op jit(solution)/shard_map/cond/branch_1_fun/all_to_all | solution.py:60
  386.4 0.1 copy.62
  386.5 13.7 %all-to-all-done.3 = bf16[32,80,128]{2,1,0:T(8,128)(2,1)S(1)} async-done(((bf16[32,80,128]{2,1,0:T(8,128)(2,1)}), bf16[32,80,128]{2,1,0:T(8,128)(2,1)S(1)}, u32[]{:S(2)}, u32[]{:S(2)}) %all-to-all-start.3) | async-done | bytes 655392 | tf_op jit(solution)/shard_map/cond/branch_1_fun/all_to_all | solution.py:60
  400.1 0.4 convolution_bitcast_fusion.3
  400.6 0.7 fusion.33
  (19 shorter events, 0.1 us)
Async XLA Ops:
  7.9 3.5 copy-start.1
  11.4 3.3 collective-permute-start
  14.7 5.6 %collective-permute-start = (bf16[16,2048]{1,0:T(8,128)(2,1)S(1)}, bf16[16,2048]{1,0:T(8,128)(2,1)S(1)}, u32[]{:S(2)}, u32[]{:S(2)}) collective-permute-start(bf16[16,2048]{1,0:T(8,128)(2,1)S(1)} %get-tuple-element.318), channel_id=1, source_target_pairs={{0,32},{32,64},{64,96},{96,128},{128,160},{160,192},{192,224},{1,3... | collective-permute-start | bytes 196616 | tf_op jit(solution)/shard_map/while/body/eval_jaxpr/ppermute | solution.py:79
  20.3 5.6 %collective-permute-start = (bf16[16,2048]{1,0:T(8,128)(2,1)S(1)}, bf16[16,2048]{1,0:T(8,128)(2,1)S(1)}, u32[]{:S(2)}, u32[]{:S(2)}) collective-permute-start(bf16[16,2048]{1,0:T(8,128)(2,1)S(1)} %get-tuple-element.318), channel_id=1, source_target_pairs={{0,32},{32,64},{64,96},{96,128},{128,160},{160,192},{192,224},{1,3... | collective-permute-start | bytes 196616 | tf_op jit(solution)/shard_map/while/body/eval_jaxpr/ppermute | solution.py:79
  25.9 5.6 %collective-permute-start = (bf16[16,2048]{1,0:T(8,128)(2,1)S(1)}, bf16[16,2048]{1,0:T(8,128)(2,1)S(1)}, u32[]{:S(2)}, u32[]{:S(2)}) collective-permute-start(bf16[16,2048]{1,0:T(8,128)(2,1)S(1)} %get-tuple-element.318), channel_id=1, source_target_pairs={{0,32},{32,64},{64,96},{96,128},{128,160},{160,192},{192,224},{1,3... | collective-permute-start | bytes 196616 | tf_op jit(solution)/shard_map/while/body/eval_jaxpr/ppermute | solution.py:79
  31.4 5.6 %collective-permute-start = (bf16[16,2048]{1,0:T(8,128)(2,1)S(1)}, bf16[16,2048]{1,0:T(8,128)(2,1)S(1)}, u32[]{:S(2)}, u32[]{:S(2)}) collective-permute-start(bf16[16,2048]{1,0:T(8,128)(2,1)S(1)} %get-tuple-element.318), channel_id=1, source_target_pairs={{0,32},{32,64},{64,96},{96,128},{128,160},{160,192},{192,224},{1,3... | collective-permute-start | bytes 196616 | tf_op jit(solution)/shard_map/while/body/eval_jaxpr/ppermute | solution.py:79
  37.0 5.6 %collective-permute-start = (bf16[16,2048]{1,0:T(8,128)(2,1)S(1)}, bf16[16,2048]{1,0:T(8,128)(2,1)S(1)}, u32[]{:S(2)}, u32[]{:S(2)}) collective-permute-start(bf16[16,2048]{1,0:T(8,128)(2,1)S(1)} %get-tuple-element.318), channel_id=1, source_target_pairs={{0,32},{32,64},{64,96},{96,128},{128,160},{160,192},{192,224},{1,3... | collective-permute-start | bytes 196616 | tf_op jit(solution)/shard_map/while/body/eval_jaxpr/ppermute | solution.py:79
  42.6 313.9 %collective-permute-start = (bf16[16,2048]{1,0:T(8,128)(2,1)S(1)}, bf16[16,2048]{1,0:T(8,128)(2,1)S(1)}, u32[]{:S(2)}, u32[]{:S(2)}) collective-permute-start(bf16[16,2048]{1,0:T(8,128)(2,1)S(1)} %get-tuple-element.318), channel_id=1, source_target_pairs={{0,32},{32,64},{64,96},{96,128},{128,160},{160,192},{192,224},{1,3... | collective-permute-start | bytes 196616 | tf_op jit(solution)/shard_map/while/body/eval_jaxpr/ppermute | solution.py:79
  382.0 18.2 %all-to-all-start.3 = ((bf16[32,80,128]{2,1,0:T(8,128)(2,1)}), bf16[32,80,128]{2,1,0:T(8,128)(2,1)S(1)}, u32[]{:S(2)}, u32[]{:S(2)}) async-start(bf16[32,80,128]{2,1,0:T(8,128)(2,1)} %copy.47), calls=%async_computation.3 | async-start | bytes 1310720 | tf_op jit(solution)/shard_map/cond/branch_1_fun/all_to_all | solution.py:60

commit v4 on v1

--- a/solution.py
+++ b/solution.py
@@ -78,7 +78,7 @@
         output, result = lax.cond(section_id == turn_index, step, lambda kept: kept, held)
         return lax.ppermute(output, "pp", ring), result
 
-    _, result = lax.fori_loop(0, sections, turn, (tokens, tokens))
+    _, result = lax.fori_loop(0, sections, turn, (tokens, tokens), unroll=2)
     return result[None]
 
 

time: 398 us -> 398 us (level)
  no operation moved by 1% of the time
where the time goes in v4:
time: 398 us
  waiting for transfers between devices  334 us (84%)
  blocking collectives  35.9 us (9%)
  starting transfers between devices  10.3 us (3%)
  local copies, waits for them, and re-layouts  9.87 us (2%)
  matrix products  5.64 us (1%)
    ppermute x8, waiting for transfers between devices, turn(): return (lax.ppermute(output, 'pp', ring), result)  334 us
    all_to_all x1, blocking collectives, layer(): lax.all_to_all(produced.astype(jnp.bfloat16).reshape(group_size, capacity...  18 us
    all_to_all x1, blocking collectives, exchange(): moved = lax.all_to_all(dense, 'ep', 0, 0, tiled=True)  18 us
    ppermute x8, starting transfers between devices, turn(): return (lax.ppermute(output, 'pp', ring), result)  10.3 us
  transfers between devices with their start and end apart: 8, of which 8 were waited for; matrix products, arithmetic and copies ran while one was open for 0% of the time, Pallas kernels for 0%

profile of v4, /device:TPU:7, one launch (start us, length us, event | category | flops | bytes accessed | tf_op | source)
XLA Modules:
  0.0 397.6 jit_solution(3289743169838992845)
XLA Ops:
  0.0 0.8 copy.100
  0.8 0.8 constant_dynamic-slice_fusion
  1.6 0.1 copy.45
  1.7 0.1 eq.49
  1.8 0.1 fusion.39
  1.9 0.2 reduce_window_sum.11
  2.0 0.2 select_reduce_fusion.1
  2.2 0.1 reduce_sum.39
  2.3 0.1 copy.46
  2.4 0.8 bitcast_add_fusion
  3.1 0.1 copy.47
  3.2 0.1 fusion.38
  3.4 0.1 copy.48
  3.5 0.1 copy.52
  3.6 3.2 copy.49
  6.8 0.0 copy-start.4
  6.8 0.0 copy-start.2
  6.8 2.8 copy.53
  9.6 0.0 copy-done.4
  9.6 0.1 copy.50
  9.7 0.1 select_reduce_fusion
  9.8 0.1 copy.51
  10.0 0.1 copy.54
  10.1 0.0 copy-done.2
  10.1 386.9 %while.17 = (s32[]{:T(128)}, bf16[16,2048]{1,0:T(8,128)(2,1)S(1)}, bf16[16,2048]{1,0:T(8,128)(2,1)S(1)}, s32[]{:T(128)}, f32[1,2048]{1,0:T(1,128)S(1)}, /*index=...) while((s32[]{:T(128)}, bf16[16,2048]{1,0:T(8,128)(2,1)S(1)}, ...), condition=%wide.region_11.12_spmd, body=%wide.region_4.11_spmd.sunk | while | flops 3170140160 | bytes 68729816 | solution.py:81
  10.1 1.3 collective-permute-start
  11.4 2.0 collective-permute-done
  13.4 1.3 collective-permute-start.1
  14.7 4.3 %collective-permute-done.1 = bf16[16,2048]{1,0:T(8,128)(2,1)S(1)} collective-permute-done((bf16[16,2048]{1,0:T(8,128)(2,1)S(1)}, bf16[16,2048]{1,0:T(8,128)(2,1)S(1)}, u32[]{:S(2)}, u32[]{:S(2)}) %collective-permute-start.1) | collective-permute-done | bytes 65568 | tf_op jit(solution)/shard_map/while/body/eval_jaxpr/ppermute | solution.py:79
  19.0 1.3 collective-permute-start
  20.3 4.3 %collective-permute-done = bf16[16,2048]{1,0:T(8,128)(2,1)S(1)} collective-permute-done((bf16[16,2048]{1,0:T(8,128)(2,1)S(1)}, bf16[16,2048]{1,0:T(8,128)(2,1)S(1)}, u32[]{:S(2)}, u32[]{:S(2)}) %collective-permute-start) | collective-permute-done | bytes 65568 | tf_op jit(solution)/shard_map/while/body/eval_jaxpr/ppermute | solution.py:79
  24.6 1.3 collective-permute-start.1
  25.9 4.3 %collective-permute-done.1 = bf16[16,2048]{1,0:T(8,128)(2,1)S(1)} collective-permute-done((bf16[16,2048]{1,0:T(8,128)(2,1)S(1)}, bf16[16,2048]{1,0:T(8,128)(2,1)S(1)}, u32[]{:S(2)}, u32[]{:S(2)}) %collective-permute-start.1) | collective-permute-done | bytes 65568 | tf_op jit(solution)/shard_map/while/body/eval_jaxpr/ppermute | solution.py:79
  30.1 1.3 collective-permute-start
  31.4 4.3 %collective-permute-done = bf16[16,2048]{1,0:T(8,128)(2,1)S(1)} collective-permute-done((bf16[16,2048]{1,0:T(8,128)(2,1)S(1)}, bf16[16,2048]{1,0:T(8,128)(2,1)S(1)}, u32[]{:S(2)}, u32[]{:S(2)}) %collective-permute-start) | collective-permute-done | bytes 65568 | tf_op jit(solution)/shard_map/while/body/eval_jaxpr/ppermute | solution.py:79
  35.7 1.3 collective-permute-start.1
  37.0 4.3 %collective-permute-done.1 = bf16[16,2048]{1,0:T(8,128)(2,1)S(1)} collective-permute-done((bf16[16,2048]{1,0:T(8,128)(2,1)S(1)}, bf16[16,2048]{1,0:T(8,128)(2,1)S(1)}, u32[]{:S(2)}, u32[]{:S(2)}) %collective-permute-start.1) | collective-permute-done | bytes 65568 | tf_op jit(solution)/shard_map/while/body/eval_jaxpr/ppermute | solution.py:79
  41.3 1.3 collective-permute-start
  42.6 308.6 %collective-permute-done = bf16[16,2048]{1,0:T(8,128)(2,1)S(1)} collective-permute-done((bf16[16,2048]{1,0:T(8,128)(2,1)S(1)}, bf16[16,2048]{1,0:T(8,128)(2,1)S(1)}, u32[]{:S(2)}, u32[]{:S(2)}) %collective-permute-start) | collective-permute-done | bytes 65568 | tf_op jit(solution)/shard_map/while/body/eval_jaxpr/ppermute | solution.py:79
  351.2 42.6 %conditional.5 = ((bf16[16,2048]{1,0:T(8,128)(2,1)S(1)}, bf16[16,2048]{1,0:T(8,128)(2,1)S(1)})) conditional(s32[]{:T(128)} %convert_element_type.133, (bf16[16,2048]{1,0:T(8,128)(2,1)S(1)}, bf16[16,2048]{1,0:T(8,128)(2,1)S(1)}) %tuple.58, (bf16[16,2048]{1,0:T(8,128)(2,1)S(1)}, f32[1,2048]{1,0:T(1,128)S(1)}, bf16[32,5,16]{0,2,1:T(8,128)(2,1)S(1)}, ...), branch_computations={%region_8.8_spmd, %region_9.10_spmd} | conditional | flops 1585070080 | bytes 34102580 | solution.py:78
  351.2 0.1 fusion.29
  351.4 0.1 fusion.33
  351.5 0.4 fusion.24
  351.8 0.3 copy.40
  352.1 18.0 %all_to_all.18 = bf16[32,80,128]{2,1,0:T(8,128)(2,1)S(1)} all-to-all(bf16[32,80,128]{2,1,0:T(8,128)(2,1)S(1)} %bitcast.100), channel_id=1, replica_groups=mesh['pp'=8,'ep'=32] {'ep'}, dimensions={0} | all-to-all | bytes 1310720 | tf_op jit(solution)/shard_map/while/body/eval_jaxpr/cond/branch_1_fun/all_to_all | solution.py:42
  370.1 0.2 copy.41
  370.2 0.0 copy-start.1
  370.3 4.1 %convolution_bitcast_fusion.2 = f32[32,5,1536]{2,0,1:T(8,128)S(1)} fusion(bf16[32,5,16,128]{3,0,2,1:T(8,128)(2,1)S(1)} %bitcast.103, bf16[16,128,1536,1]{2,1,0,3:T(8,128)(2,1)} %bitcast.97), kind=kOutput, calls=%fused_computation.26 | convolution fusion | flops 1006632960 | bytes 7929856 | tf_op jit(solution)/shard_map/while/body/eval_jaxpr/cond/branch_1_fun/gcjk,jkh->gch/dot_general | solution.py:53
  374.4 0.0 copy-done.1
  374.4 0.7 fusion.21
  375.1 0.3 copy.42
  375.4 18.0 %all_to_all.19 = bf16[32,80,128]{2,1,0:T(8,128)(2,1)S(1)} all-to-all(bf16[32,80,128]{2,1,0:T(8,128)(2,1)S(1)} %copy.42), channel_id=1, replica_groups=mesh['pp'=8,'ep'=32] {'ep'}, dimensions={0} | all-to-all | bytes 1310720 | tf_op jit(solution)/shard_map/while/body/eval_jaxpr/cond/branch_1_fun/all_to_all | solution.py:60
  393.4 0.4 convolution_bitcast_fusion.3
  393.8 1.3 collective-permute-start.1
  395.1 1.8 collective-permute-done.1
  397.0 0.0 copy-start.3
  397.0 0.6 copy-done.3
  (15 shorter events, 0.1 us)
Async XLA Ops:
  6.8 2.8 copy-start.4
  6.8 3.2 copy-start.2
  10.1 3.3 collective-permute-start
  13.4 5.6 %collective-permute-start.1 = (bf16[16,2048]{1,0:T(8,128)(2,1)S(1)}, bf16[16,2048]{1,0:T(8,128)(2,1)S(1)}, u32[]{:S(2)}, u32[]{:S(2)}) collective-permute-start(bf16[16,2048]{1,0:T(8,128)(2,1)S(1)} %get-tuple-element.384), channel_id=1, source_target_pairs={{0,32},{32,64},{64,96},{96,128},{128,160},{160,192},{192,224},{1,3... | collective-permute-start | bytes 196616 | tf_op jit(solution)/shard_map/while/body/eval_jaxpr/ppermute | solution.py:79
  19.0 5.6 %collective-permute-start = (bf16[16,2048]{1,0:T(8,128)(2,1)S(1)}, bf16[16,2048]{1,0:T(8,128)(2,1)S(1)}, u32[]{:S(2)}, u32[]{:S(2)}) collective-permute-start(bf16[16,2048]{1,0:T(8,128)(2,1)S(1)} %get-tuple-element.382), channel_id=1, source_target_pairs={{0,32},{32,64},{64,96},{96,128},{128,160},{160,192},{192,224},{1,3... | collective-permute-start | bytes 196616 | tf_op jit(solution)/shard_map/while/body/eval_jaxpr/ppermute | solution.py:79
  24.6 5.6 %collective-permute-start.1 = (bf16[16,2048]{1,0:T(8,128)(2,1)S(1)}, bf16[16,2048]{1,0:T(8,128)(2,1)S(1)}, u32[]{:S(2)}, u32[]{:S(2)}) collective-permute-start(bf16[16,2048]{1,0:T(8,128)(2,1)S(1)} %get-tuple-element.384), channel_id=1, source_target_pairs={{0,32},{32,64},{64,96},{96,128},{128,160},{160,192},{192,224},{1,3... | collective-permute-start | bytes 196616 | tf_op jit(solution)/shard_map/while/body/eval_jaxpr/ppermute | solution.py:79
  30.1 5.6 %collective-permute-start = (bf16[16,2048]{1,0:T(8,128)(2,1)S(1)}, bf16[16,2048]{1,0:T(8,128)(2,1)S(1)}, u32[]{:S(2)}, u32[]{:S(2)}) collective-permute-start(bf16[16,2048]{1,0:T(8,128)(2,1)S(1)} %get-tuple-element.382), channel_id=1, source_target_pairs={{0,32},{32,64},{64,96},{96,128},{128,160},{160,192},{192,224},{1,3... | collective-permute-start | bytes 196616 | tf_op jit(solution)/shard_map/while/body/eval_jaxpr/ppermute | solution.py:79
  35.7 5.6 %collective-permute-start.1 = (bf16[16,2048]{1,0:T(8,128)(2,1)S(1)}, bf16[16,2048]{1,0:T(8,128)(2,1)S(1)}, u32[]{:S(2)}, u32[]{:S(2)}) collective-permute-start(bf16[16,2048]{1,0:T(8,128)(2,1)S(1)} %get-tuple-element.384), channel_id=1, source_target_pairs={{0,32},{32,64},{64,96},{96,128},{128,160},{160,192},{192,224},{1,3... | collective-permute-start | bytes 196616 | tf_op jit(solution)/shard_map/while/body/eval_jaxpr/ppermute | solution.py:79
  41.3 309.9 %collective-permute-start = (bf16[16,2048]{1,0:T(8,128)(2,1)S(1)}, bf16[16,2048]{1,0:T(8,128)(2,1)S(1)}, u32[]{:S(2)}, u32[]{:S(2)}) collective-permute-start(bf16[16,2048]{1,0:T(8,128)(2,1)S(1)} %get-tuple-element.382), channel_id=1, source_target_pairs={{0,32},{32,64},{64,96},{96,128},{128,160},{160,192},{192,224},{1,3... | collective-permute-start | bytes 196616 | tf_op jit(solution)/shard_map/while/body/eval_jaxpr/ppermute | solution.py:79
  370.2 4.1 %copy-start.1 = (bf16[768,16,128]{2,0,1:T(8,128)(2,1)S(1)}, bf16[768,16,128]{2,0,1:T(8,128)(2,1)}, u32[]{:S(2)}) copy-start(bf16[768,16,128]{2,0,1:T(8,128)(2,1)} %get-tuple-element.269) | copy-start | bytes 9437188 | tf_op jit(solution)/shard_map/while/body/eval_jaxpr/cond
  393.8 3.1 collective-permute-start.1
  397.0 0.6 copy-start.3
